TPU v7x, 128 devices: a whole 4x4x4 slice. The times are simulated.
128 devices in a mesh: sector: 8 (over y, core), row: 16 (over x, z).
Axes of the slice: x: 4, y: 4, z: 4, core: 2. Of those that a mesh axis runs over, the one named last changes fastest.
Arguments:
- amplitudes: bfloat16 [8192, 4, 8192], P('sector', None, 'row'), may hold values from -6 to 6
- next_site: bfloat16 [8, 4, 8192, 2048], P('sector', None, 'row'), may hold values from -0.03125 to 0.03125
- sector_rows: int32 [8], replicated, may hold values from 512 to 1024, as said below
- moves: int32 [2, 8], replicated, may hold values from 0 to 128, as said below
- angles: float32 [2, 8, 128], replicated, may hold values from -3.140625 to 3.140625
- ranks: int32 [8], replicated, may hold values from 256 to 1024, as said below
Outputs:
- canonical: bfloat16 [2048, 8192], P('row', 'sector')
Inputs may be any that keep to these rules, and one draw needn't show every extreme that they name: `sector_rows`: one sector has exactly 1024 live rows and another exactly 512. `moves`: the entry of the last sector is 0, every other entry is 1 or more; for each gate some pair moves exactly 128 rows. `ranks`: each sector keeps at least half of its live rows and at most all of them; one sector keeps 1024 rows and one keeps 1024 // 4.
All inputs are finite; a program needn't handle non-finite values.
Results may differ from a plain program's by a relative error of at most 0.014.
Values may be sent and summed in bfloat16 or wider, within the bound.
No kernel may reach another device: no remote copies, remote signals or barrier semaphores. Data moves between devices by JAX's collectives and lax.ppermute only.
A program may use at most 128 MiB of HBM per device.

v0:
```python
import math
import jax
import jax.numpy as jnp
from jax import lax
from jax.sharding import PartitionSpec as P

KOUT = 2048


def shifted(x, axis, by):
    size = lax.axis_size(axis)
    pairs = [(i, i + by) for i in range(size) if 0 <= i + by < size]
    return lax.ppermute(x, axis, pairs)


def rotate_rows(
    padded, start_a, start_b, from_above, from_below, angle_here, angle_prev, count_here, count_prev
):
    slot_count = from_above.shape[0]
    slot_index = jnp.arange(slot_count)
    rows_a = lax.dynamic_slice_in_dim(padded, start_a, slot_count, 0)
    rows_b = lax.dynamic_slice_in_dim(padded, start_b, slot_count, 0)
    above_rows = from_above.astype(jnp.float32)
    below_rows = from_below.astype(jnp.float32)
    cos_here = jnp.cos(angle_here)[:, None, None]
    sin_here = jnp.sin(angle_here)[:, None, None]
    cos_prev = jnp.cos(angle_prev)[:, None, None]
    sin_prev = jnp.sin(angle_prev)[:, None, None]
    new_a = jnp.where(
        (slot_index < count_here)[:, None, None], cos_here * rows_a - sin_here * above_rows, rows_a
    )
    new_b = jnp.where(
        (slot_index < count_prev)[:, None, None], sin_prev * below_rows + cos_prev * rows_b, rows_b
    )
    padded = lax.dynamic_update_slice_in_dim(padded, new_a, start_a, 0)
    return lax.dynamic_update_slice_in_dim(padded, new_b, start_b, 0)


def per_device(amplitudes, next_site, sector_rows, moves, angles, ranks):
    sector_id = lax.axis_index("sector")
    sector_rows_count = amplitudes.shape[0]
    move_rows = sector_rows_count // 8
    row_index = jnp.arange(sector_rows_count)
    live_rows = sector_rows[sector_id]
    prev_id = jnp.maximum(sector_id - 1, 0)
    count_here = moves[:, sector_id]
    count_prev = jnp.where(sector_id > 0, moves[:, prev_id], 0)
    local_rows = jnp.where(
        (row_index < live_rows)[:, None, None], amplitudes.astype(jnp.float32), 0.0
    )
    tail_zeros = jnp.zeros((move_rows,) + local_rows.shape[1:], jnp.float32)
    padded = jnp.concatenate([local_rows, tail_zeros], 0)
    starts_a = [live_rows - count_here[0], live_rows - count_here[0] - count_here[1]]
    starts_b = [jnp.int32(0), count_prev[0]]
    for gate_index in range(2):
        send_up = lax.dynamic_slice_in_dim(padded, starts_a[gate_index], move_rows, 0).astype(
            jnp.bfloat16
        )
        send_down = lax.dynamic_slice_in_dim(padded, starts_b[gate_index], move_rows, 0).astype(
            jnp.bfloat16
        )
        from_below = shifted(send_up, "sector", 1)
        from_above = shifted(send_down, "sector", -1)
        padded = rotate_rows(
            padded,
            starts_a[gate_index],
            starts_b[gate_index],
            from_above,
            from_below,
            angles[gate_index][sector_id],
            angles[gate_index][prev_id],
            count_here[gate_index],
            count_prev[gate_index],
        )
    block_rows = padded[:sector_rows_count].astype(jnp.bfloat16)
    site_tensor = next_site[0]
    contracted = lax.psum_scatter(
        jnp.einsum("prk,lpr->kl", site_tensor, block_rows, preferred_element_type=jnp.float32),
        "row",
        scatter_dimension=0,
        tiled=True,
    ).astype(jnp.bfloat16)
    local_gram = lax.dot_general(
        contracted, contracted, (((0,), (0,)), ((), ())), preferred_element_type=jnp.float32
    )
    gram_matrix = lax.psum(local_gram, "row")
    dead_rows = (row_index >= live_rows).astype(jnp.float32)
    gram_matrix = gram_matrix + jnp.diag(dead_rows)
    factor_low = jnp.linalg.cholesky(gram_matrix)
    solved = jax.scipy.linalg.solve_triangular(
        factor_low, contracted.astype(jnp.float32).T, lower=True
    ).T
    kept_mask = ((row_index >= live_rows - ranks[sector_id]) & (row_index < live_rows)).astype(
        jnp.float32
    )
    return (solved * math.sqrt(KOUT) * kept_mask[None, :]).astype(jnp.bfloat16)


def solution(mesh):
    placed = (P("sector", None, "row"), P("sector", None, "row", None), P(), P(), P(), P())
    return jax.shard_map(
        per_device, mesh=mesh, in_specs=placed, out_specs=P("row", "sector"), check_vma=False
    )
```

profile of v0, /device:TPU:1, one launch (start us, length us, event | category | flops | bytes accessed | tf_op | source)
XLA Modules:
  0.0 640.3 jit_solution(2084765456773674766)
XLA Ops:
  27.3 8.1 %concatenate.30 = f32[1152,4,512]{2,0,1:T(8,128)} pad(f32[1024,4,512]{2,0,1:T(8,128)} %copy-done, f32[]{:T(128)} %constant.290.clone.1), padding=0_128x0_0x0_0 | pad | bytes 17825796 | tf_op jit(solution)/shard_map/concatenate | solution.py:52
  38.4 5.9 dynamic_update_slice.12
  62.6 5.9 dynamic_update_slice.14
  68.5 5.9 dynamic_update_slice.15
  74.4 15.6 %fusion.2 = f32[2048,1024]{0,1:T(8,128)} fusion(bf16[1,4,512,2048]{3,2,1,0:T(8,128)(2,1)} %param.7, f32[1152,4,512]{2,0,1:T(8,128)} %dynamic_update_slice.15), kind=kOutput, calls=%fused_computation.7 | convolution fusion | flops 8589934592 | bytes 20971520 | tf_op jit(solution)/shard_map/prk,lpr->kl/dot_general | solution.py:78
  90.1 87.1 %reduce-scatter.2.cloned.1.call-done = f32[128,1024]{0,1:T(8,128)} async-done(((f32[2048,1024]{0,1:T(8,128)}), f32[128,1024]{0,1:T(8,128)}) %reduce-scatter.2.cloned.1.call-update) | async-done | bytes 524304 | tf_op jit(solution)/shard_map/reduce_scatter | solution.py:77
  184.3 100.9 %all-reduce.4.cloned.1.call-done = f32[1024,1024]{0,1:T(8,128)} async-done(((f32[1024,1024]{0,1:T(8,128)}), f32[1024,1024]{0,1:T(8,128)}) %all-reduce.4.cloned.1.call-update) | async-done | bytes 4194320 | tf_op jit(solution)/shard_map/psum | solution.py:86
  302.2 11.7 %cholesky.222 = f32[128,128]{1,0:T(8,128)S(1)} custom-call(f32[128,128]{1,0:T(8,128)S(1)} %cholesky.577), custom_call_target="Cholesky" | custom-call | tf_op jit(solution)/shard_map/jit(cholesky)/cholesky | solution.py:89
  314.0 9.8 %custom-call.63 = f32[1,128,128]{1,2,0:T(8,128)S(1)} custom-call(f32[1,128,128]{2,1,0:T(8,128)S(1)} %get-tuple-element.73), custom_call_target="InvertDiagBlocksLowerTriangular" | custom-call | tf_op jit(solution)/shard_map/jit(cholesky)/cholesky | solution.py:89
  326.9 11.7 %cholesky.243 = f32[128,128]{1,0:T(8,128)S(1)} custom-call(f32[128,128]{1,0:T(8,128)S(1)} %cholesky.581), custom_call_target="Cholesky" | custom-call | tf_op jit(solution)/shard_map/jit(cholesky)/cholesky | solution.py:89
  341.7 9.8 %custom-call.64 = f32[1,128,128]{1,2,0:T(8,128)S(1)} custom-call(f32[1,128,128]{2,1,0:T(8,128)S(1)} %get-tuple-element.71), custom_call_target="InvertDiagBlocksLowerTriangular" | custom-call | tf_op jit(solution)/shard_map/jit(cholesky)/cholesky | solution.py:89
  357.0 11.7 %cholesky.466 = f32[128,128]{1,0:T(8,128)S(1)} custom-call(f32[128,128]{1,0:T(8,128)S(1)} %cholesky.586), custom_call_target="Cholesky" | custom-call | tf_op jit(solution)/shard_map/jit(cholesky)/cholesky | solution.py:89
  369.5 9.8 %custom-call.65 = f32[1,128,128]{1,2,0:T(8,128)S(1)} custom-call(f32[1,128,128]{2,1,0:T(8,128)S(1)} %get-tuple-element.69), custom_call_target="InvertDiagBlocksLowerTriangular" | custom-call | tf_op jit(solution)/shard_map/jit(cholesky)/cholesky | solution.py:89
  383.9 11.7 %cholesky.485 = f32[128,128]{1,0:T(8,128)S(1)} custom-call(f32[128,128]{1,0:T(8,128)S(1)} %cholesky.591), custom_call_target="Cholesky" | custom-call | tf_op jit(solution)/shard_map/jit(cholesky)/cholesky | solution.py:89
  396.4 9.8 %custom-call.66 = f32[1,128,128]{1,2,0:T(8,128)S(1)} custom-call(f32[1,128,128]{2,1,0:T(8,128)S(1)} %get-tuple-element.67), custom_call_target="InvertDiagBlocksLowerTriangular" | custom-call | tf_op jit(solution)/shard_map/jit(cholesky)/cholesky | solution.py:89
  410.5 12.1 %cholesky.504 = f32[128,128]{1,0:T(8,128)S(1)} custom-call(f32[128,128]{1,0:T(8,128)S(1)} %cholesky.596), custom_call_target="Cholesky" | custom-call | tf_op jit(solution)/shard_map/jit(cholesky)/cholesky | solution.py:89
  423.4 9.8 %custom-call.67 = f32[1,128,128]{1,2,0:T(8,128)S(1)} custom-call(f32[1,128,128]{2,1,0:T(8,128)S(1)} %get-tuple-element.65), custom_call_target="InvertDiagBlocksLowerTriangular" | custom-call | tf_op jit(solution)/shard_map/jit(cholesky)/cholesky | solution.py:89
  437.4 11.7 %cholesky.524 = f32[128,128]{1,0:T(8,128)S(1)} custom-call(f32[128,128]{1,0:T(8,128)S(1)} %cholesky.601), custom_call_target="Cholesky" | custom-call | tf_op jit(solution)/shard_map/jit(cholesky)/cholesky | solution.py:89
  449.9 9.8 %custom-call.68 = f32[1,128,128]{1,2,0:T(8,128)S(1)} custom-call(f32[1,128,128]{2,1,0:T(8,128)S(1)} %get-tuple-element.63), custom_call_target="InvertDiagBlocksLowerTriangular" | custom-call | tf_op jit(solution)/shard_map/jit(cholesky)/cholesky | solution.py:89
  463.5 11.7 %cholesky.544 = f32[128,128]{1,0:T(8,128)S(1)} custom-call(f32[128,128]{1,0:T(8,128)S(1)} %cholesky.606), custom_call_target="Cholesky" | custom-call | tf_op jit(solution)/shard_map/jit(cholesky)/cholesky | solution.py:89
  476.0 9.8 %custom-call.69 = f32[1,128,128]{1,2,0:T(8,128)S(1)} custom-call(f32[1,128,128]{2,1,0:T(8,128)S(1)} %get-tuple-element.61), custom_call_target="InvertDiagBlocksLowerTriangular" | custom-call | tf_op jit(solution)/shard_map/jit(cholesky)/cholesky | solution.py:89
  488.9 11.7 %cholesky.562 = f32[128,128]{1,0:T(8,128)S(1)} custom-call(f32[128,128]{1,0:T(8,128)S(1)} %convolution_subtract_fusion.11), custom_call_target="Cholesky" | custom-call | tf_op jit(solution)/shard_map/jit(cholesky)/cholesky | solution.py:89
  516.5 23.7 %while.1 = (s32[]{:T(128)}, f32[1024,1024]{0,1:T(8,128)}, s32[8,2]{0,1:T(2,128)S(1)}, f32[8,128,128]{2,1,0:T(8,128)S(1)}, s32[]{:T(128)}) while((s32[]{:T(128)}, f32[1024,1024]{0,1:T(8,128)}, s32[8,2]{0,1:T(2,128)S(1)}, f32[8,128,128]{2,1,0:T(8,128)S(1)}, s32[]{:T(128)}) %tuple.65), condition=%wide.while_cond, body=%wide.while_body.sunk | while | flops 2 | bytes 393321 | solution.py:90
  540.3 78.8 %custom-call.70 = f32[8,128,128]{1,2,0:T(8,128)S(1)} custom-call(f32[8,128,128]{2,1,0:T(8,128)S(1)} %get-tuple-element.12), custom_call_target="InvertDiagBlocksLowerTriangular" | custom-call | tf_op jit(solution)/shard_map/jit(_solve_triangular)/triangular_solve | solution.py:90
  (163 shorter events, 144.8 us)
Async XLA Ops:
  6.5 170.7 %reduce-scatter.2.cloned.1.call-start = ((), (), s32[]{:S(2)}) async-start(), calls=%async_computation.1 | async-start | bytes 8912896 | tf_op jit(solution)/shard_map/reduce_scatter | solution.py:77
  14.9 3.3 copy-start
  14.9 9.8 %copy-start.3 = (f32[2,8,128]{2,1,0:T(8,128)S(1)}, f32[2,8,128]{2,1,0:T(8,128)}, u32[]{:S(2)}) copy-start(f32[2,8,128]{2,1,0:T(8,128)} %param.10) | copy-start | bytes 24580
  18.2 18.6 %collective-permute-start = (bf16[128,4,512]{2,0,1:T(8,128)(2,1)S(1)}, bf16[128,4,512]{2,0,1:T(8,128)(2,1)S(1)}, u32[]{:S(2)}, u32[]{:S(2)}) collective-permute-start(bf16[128,4,512]{2,0,1:T(8,128)(2,1)S(1)} %get-tuple-element.34), channel_id=1, source_target_pairs={{16,0},{32,16},{48,32},{64,48},{80,64},{96,80},{112,96},{17,1},{33... | collective-permute-start | bytes 1572872 | tf_op jit(solution)/shard_map/ppermute | solution.py:13
  21.5 22.8 %collective-permute-start.1 = (bf16[128,4,512]{2,0,1:T(8,128)(2,1)S(1)}, bf16[128,4,512]{2,0,1:T(8,128)(2,1)S(1)}, u32[]{:S(2)}, u32[]{:S(2)}) collective-permute-start(bf16[128,4,512]{2,0,1:T(8,128)(2,1)S(1)} %get-tuple-element.33), channel_id=1, source_target_pairs={{0,16},{16,32},{32,48},{48,64},{64,80},{80,96},{96,112},{1,17},{17... | collective-permute-start | bytes 1572872 | tf_op jit(solution)/shard_map/ppermute | solution.py:13
  48.7 10.5 %collective-permute-start.2 = (bf16[128,4,512]{2,0,1:T(8,128)(2,1)S(1)}, bf16[128,4,512]{2,0,1:T(8,128)(2,1)S(1)}, u32[]{:S(2)}, u32[]{:S(2)}) collective-permute-start(bf16[128,4,512]{2,0,1:T(8,128)(2,1)S(1)} %get-tuple-element.32), channel_id=1, source_target_pairs={{16,0},{32,16},{48,32},{64,48},{80,64},{96,80},{112,96},{17,1},{33... | collective-permute-start | bytes 1572872 | tf_op jit(solution)/shard_map/ppermute | solution.py:13
  50.6 9.8 %collective-permute-start.3 = (bf16[128,4,512]{2,0,1:T(8,128)(2,1)S(1)}, bf16[128,4,512]{2,0,1:T(8,128)(2,1)S(1)}, u32[]{:S(2)}, u32[]{:S(2)}) collective-permute-start(bf16[128,4,512]{2,0,1:T(8,128)(2,1)S(1)} %get-tuple-element.31), channel_id=1, source_target_pairs={{0,16},{16,32},{32,48},{48,64},{64,80},{80,96},{96,112},{1,17},{17... | collective-permute-start | bytes 1572872 | tf_op jit(solution)/shard_map/ppermute | solution.py:13
  90.0 91.2 %copy-start.4 = (s32[8]{0:T(128)S(1)}, s32[8]{0:T(128)}, u32[]{:S(2)}) copy-start(s32[8]{0:T(128)} %param.11) | copy-start | bytes 100
  90.0 195.1 %all-reduce.4.cloned.1.call-start = ((), (), s32[]{:S(2)}) async-start(), calls=%async_computation.2 | async-start | bytes 8388608 | tf_op jit(solution)/shard_map/psum | solution.py:86
  177.2 7.0 %copy-start.2 = (f32[128,1024]{0,1:T(8,128)S(1)}, f32[128,1024]{0,1:T(8,128)}, u32[]{:S(2)}) copy-start(f32[128,1024]{0,1:T(8,128)} %reduce-scatter.2.cloned.1.call-done) | copy-start | bytes 1572868
  300.3 1.9 copy-start.1
Sparse Core Ops, SparseCore 0:
  90.1 87.0 reduce-scatter.1
  181.3 103.8 all-reduce.3
where the time goes:
time: 650 us; the launch traced here: 640 us
  other arithmetic  277 us (43%)
  waiting for transfers between devices  193 us (30%)
  local copies, waits for them, and re-layouts  74.6 us (11%)
  matrix products  59.6 us (9%)
  between operations  24.2 us (4%)
  starting transfers between devices  12.1 us (2%)
    another operation x31, other arithmetic, per_device(): factor_low = jnp.linalg.cholesky(gram_matrix)  168 us
    psum x1, waiting for transfers between devices, per_device(): gram_matrix = lax.psum(local_gram, 'row')  101 us
    reduce_scatter x1, waiting for transfers between devices, per_device(): lax.psum_scatter(jnp.einsum('prk,lpr->kl', site_tensor, block_rows, prefe...  87.1 us
    another operation x3, other arithmetic, per_device(): jax.scipy.linalg.solve_triangular(factor_low, contracted.astype(jnp.float...  83.6 us
    another operation x14, matrix products, per_device(): factor_low = jnp.linalg.cholesky(gram_matrix)  27 us
    another operation x40, local copies, waits for them, and re-layouts  23.5 us
    dot_general x1, matrix products, per_device(): jnp.einsum('prk,lpr->kl', site_tensor, block_rows, preferred_element_type...  15.6 us
    another operation x15, matrix products, per_device(): jax.scipy.linalg.solve_triangular(factor_low, contracted.astype(jnp.float...  13 us
  transfers between devices with their start and end apart: 6, of which 4 were waited for; matrix products, arithmetic and copies ran while one was open for 3% of the time, Pallas kernels for 0%

commit v1 on v0

--- a/solution.py
+++ b/solution.py
@@ -83,7 +83,7 @@
     local_gram = lax.dot_general(
         contracted, contracted, (((0,), (0,)), ((), ())), preferred_element_type=jnp.float32
     )
-    gram_matrix = lax.psum(local_gram, "row")
+    gram_matrix = jnp.sum(lax.all_gather(local_gram, "row"), axis=0)
     dead_rows = (row_index >= live_rows).astype(jnp.float32)
     gram_matrix = gram_matrix + jnp.diag(dead_rows)
     factor_low = jnp.linalg.cholesky(gram_matrix)

time: 650 us -> 925 us (1.42)
  waiting for transfers between devices: 193 us -> 458 us
  other arithmetic: 277 us -> 300 us
    all_gather x0 -> x1, waiting for transfers between devices: none -> 366 us  [per_device(): gram_matrix = jnp.sum(lax.all_gather(local_gram, 'row'), axis=0)]
    psum x1 -> x0, waiting for transfers between devices: 101 us -> none  [per_device(): gram_matrix = lax.psum(local_gram, 'row')]
    reduce_sum x0 -> x1, other arithmetic: none -> 22.9 us  [per_device(): gram_matrix = jnp.sum(lax.all_gather(local_gram, 'row'), axis=0)]
    another operation x40 -> x24, local copies, waits for them, and re-layouts: 23.5 us -> 22.7 us
  transfers between devices with their start and end apart: 6 -> 6, of which waited for: 4 -> 4; matrix products, arithmetic and copies ran while one was open for 3% -> 2% of each run, Pallas kernels for 0% -> 0%
where the time goes in v1:
time: 925 us; the launch traced here: 916 us
  waiting for transfers between devices  458 us (50%)
  other arithmetic  300 us (32%)
  local copies, waits for them, and re-layouts  67.5 us (7%)
  matrix products  54.2 us (6%)
  between operations  24.2 us (3%)
  starting transfers between devices  12.1 us (1%)
    all_gather x1, waiting for transfers between devices, per_device(): gram_matrix = jnp.sum(lax.all_gather(local_gram, 'row'), axis=0)  366 us
    another operation x31, other arithmetic, per_device(): factor_low = jnp.linalg.cholesky(gram_matrix)  173 us
    reduce_scatter x1, waiting for transfers between devices, per_device(): lax.psum_scatter(jnp.einsum('prk,lpr->kl', site_tensor, block_rows, prefe...  87.2 us
    another operation x3, other arithmetic, per_device(): jax.scipy.linalg.solve_triangular(factor_low, contracted.astype(jnp.float...  83.6 us
    another operation x14, matrix products, per_device(): factor_low = jnp.linalg.cholesky(gram_matrix)  23.1 us
    reduce_sum x1, other arithmetic, per_device(): gram_matrix = jnp.sum(lax.all_gather(local_gram, 'row'), axis=0)  22.9 us
    another operation x24, local copies, waits for them, and re-layouts  22.7 us
  transfers between devices with their start and end apart: 6, of which 4 were waited for; matrix products, arithmetic and copies ran while one was open for 2% of the time, Pallas kernels for 0%

profile of v1, /device:TPU:1, one launch (start us, length us, event | category | flops | bytes accessed | tf_op | source)
XLA Modules:
  0.0 916.0 jit_solution(9308460949941286934)
XLA Ops:
  27.6 8.1 concatenate.30
  38.6 5.9 dynamic_update_slice.12
  62.7 5.9 dynamic_update_slice.14
  74.6 15.6 %fusion.2 = f32[2048,1024]{0,1:T(8,128)} fusion(bf16[1,4,512,2048]{3,2,1,0:T(8,128)(2,1)} %param.7, f32[1152,4,512]{2,0,1:T(8,128)} %dynamic_update_slice.15), kind=kOutput, calls=%fused_computation.7 | convolution fusion | flops 8589934592 | bytes 20971520 | tf_op jit(solution)/shard_map/prk,lpr->kl/dot_general | solution.py:78
  90.3 87.2 %reduce-scatter.2.cloned.1.call-done = f32[128,1024]{0,1:T(8,128)} async-done(((f32[2048,1024]{0,1:T(8,128)}), f32[128,1024]{0,1:T(8,128)}) %reduce-scatter.2.cloned.1.call-update) | async-done | bytes 524304 | tf_op jit(solution)/shard_map/reduce_scatter | solution.py:77
  184.6 366.2 %all-gather.3.cloned.1.call-done = f32[16384,1024]{1,0:T(8,128)} async-done(((f32[1024,1024]{1,0:T(8,128)}), f32[16384,1024]{1,0:T(8,128)}) %all-gather.3.cloned.1.call-update) | async-done | bytes 67108880 | tf_op jit(solution)/shard_map/all_gather | solution.py:86
  550.9 22.9 %reduce_sum.11 = f32[1024,1024]{1,0:T(8,128)} reduce(f32[16,1024,1024]{2,1,0:T(8,128)} %bitcast.16, f32[]{:T(128)} %constant.290.clone.1), dimensions={0}, to_apply=%region_1.2 | reduce | flops 15728640 | bytes 71303168 | tf_op jit(solution)/shard_map/reduce_sum | solution.py:86
  586.1 11.7 %cholesky.222 = f32[128,128]{1,0:T(8,128)S(1)} custom-call(f32[128,128]{1,0:T(8,128)S(1)} %cholesky.577), custom_call_target="Cholesky" | custom-call | tf_op jit(solution)/shard_map/jit(cholesky)/cholesky | solution.py:89
  600.4 9.8 %custom-call.63 = f32[1,128,128]{1,2,0:T(8,128)S(1)} custom-call(f32[1,128,128]{2,1,0:T(8,128)S(1)} %get-tuple-element.77), custom_call_target="InvertDiagBlocksLowerTriangular" | custom-call | tf_op jit(solution)/shard_map/jit(cholesky)/cholesky | solution.py:89
  614.1 11.8 %cholesky.243 = f32[128,128]{1,0:T(8,128)S(1)} custom-call(f32[128,128]{1,0:T(8,128)S(1)} %cholesky.581), custom_call_target="Cholesky" | custom-call | tf_op jit(solution)/shard_map/jit(cholesky)/cholesky | solution.py:89
  627.9 9.8 %custom-call.64 = f32[1,128,128]{1,2,0:T(8,128)S(1)} custom-call(f32[1,128,128]{2,1,0:T(8,128)S(1)} %get-tuple-element.74), custom_call_target="InvertDiagBlocksLowerTriangular" | custom-call | tf_op jit(solution)/shard_map/jit(cholesky)/cholesky | solution.py:89
  641.0 11.7 %cholesky.466 = f32[128,128]{1,0:T(8,128)S(1)} custom-call(f32[128,128]{1,0:T(8,128)S(1)} %cholesky.586), custom_call_target="Cholesky" | custom-call | tf_op jit(solution)/shard_map/jit(cholesky)/cholesky | solution.py:89
  654.0 9.8 %custom-call.65 = f32[1,128,128]{1,2,0:T(8,128)S(1)} custom-call(f32[1,128,128]{2,1,0:T(8,128)S(1)} %get-tuple-element.71), custom_call_target="InvertDiagBlocksLowerTriangular" | custom-call | tf_op jit(solution)/shard_map/jit(cholesky)/cholesky | solution.py:89
  667.4 11.9 %cholesky.485 = f32[128,128]{1,0:T(8,128)S(1)} custom-call(f32[128,128]{1,0:T(8,128)S(1)} %cholesky.591), custom_call_target="Cholesky" | custom-call | tf_op jit(solution)/shard_map/jit(cholesky)/cholesky | solution.py:89
  680.6 9.8 %custom-call.66 = f32[1,128,128]{1,2,0:T(8,128)S(1)} custom-call(f32[1,128,128]{2,1,0:T(8,128)S(1)} %get-tuple-element.68), custom_call_target="InvertDiagBlocksLowerTriangular" | custom-call | tf_op jit(solution)/shard_map/jit(cholesky)/cholesky | solution.py:89
  693.8 11.7 %cholesky.504 = f32[128,128]{1,0:T(8,128)S(1)} custom-call(f32[128,128]{1,0:T(8,128)S(1)} %cholesky.596), custom_call_target="Cholesky" | custom-call | tf_op jit(solution)/shard_map/jit(cholesky)/cholesky | solution.py:89
  706.8 10.2 %custom-call.67 = f32[1,128,128]{1,2,0:T(8,128)S(1)} custom-call(f32[1,128,128]{2,1,0:T(8,128)S(1)} %get-tuple-element.65), custom_call_target="InvertDiagBlocksLowerTriangular" | custom-call | tf_op jit(solution)/shard_map/jit(cholesky)/cholesky | solution.py:89
  720.3 11.7 %cholesky.524 = f32[128,128]{1,0:T(8,128)S(1)} custom-call(f32[128,128]{1,0:T(8,128)S(1)} %cholesky.601), custom_call_target="Cholesky" | custom-call | tf_op jit(solution)/shard_map/jit(cholesky)/cholesky | solution.py:89
  733.3 9.8 %custom-call.68 = f32[1,128,128]{1,2,0:T(8,128)S(1)} custom-call(f32[1,128,128]{2,1,0:T(8,128)S(1)} %get-tuple-element.62), custom_call_target="InvertDiagBlocksLowerTriangular" | custom-call | tf_op jit(solution)/shard_map/jit(cholesky)/cholesky | solution.py:89
  746.1 11.9 %cholesky.544 = f32[128,128]{1,0:T(8,128)S(1)} custom-call(f32[128,128]{1,0:T(8,128)S(1)} %cholesky.606), custom_call_target="Cholesky" | custom-call | tf_op jit(solution)/shard_map/jit(cholesky)/cholesky | solution.py:89
  759.3 9.8 %custom-call.69 = f32[1,128,128]{1,2,0:T(8,128)S(1)} custom-call(f32[1,128,128]{2,1,0:T(8,128)S(1)} %get-tuple-element.59), custom_call_target="InvertDiagBlocksLowerTriangular" | custom-call | tf_op jit(solution)/shard_map/jit(cholesky)/cholesky | solution.py:89
  771.8 11.7 %cholesky.562 = f32[128,128]{1,0:T(8,128)S(1)} custom-call(f32[128,128]{1,0:T(8,128)S(1)} %convolution_subtract_fusion.11), custom_call_target="Cholesky" | custom-call | tf_op jit(solution)/shard_map/jit(cholesky)/cholesky | solution.py:89
  794.6 22.8 %while.1 = (s32[]{:T(128)}, f32[1024,1024]{1,0:T(8,128)}, s32[8,2]{0,1:T(2,128)S(1)}, f32[8,128,128]{2,1,0:T(8,128)S(1)}, s32[]{:T(128)}) while((s32[]{:T(128)}, f32[1024,1024]{1,0:T(8,128)}, s32[8,2]{0,1:T(2,128)S(1)}, f32[8,128,128]{2,1,0:T(8,128)S(1)}, s32[]{:T(128)}) %tuple.72), condition=%wide.while_cond, body=%wide.while_body.sunk | while | flops 2 | bytes 131181 | solution.py:90
  817.4 78.8 %custom-call.70 = f32[8,128,128]{1,2,0:T(8,128)S(1)} custom-call(f32[8,128,128]{2,1,0:T(8,128)S(1)} %get-tuple-element.12), custom_call_target="InvertDiagBlocksLowerTriangular" | custom-call | tf_op jit(solution)/shard_map/jit(_solve_triangular)/triangular_solve | solution.py:90
  (130 shorter events, 137.7 us)
Async XLA Ops:
  6.5 170.9 %reduce-scatter.2.cloned.1.call-start = ((), (), s32[]{:S(2)}) async-start(), calls=%async_computation.1 | async-start | bytes 8912896 | tf_op jit(solution)/shard_map/reduce_scatter | solution.py:77
  15.1 3.3 copy-start
  15.1 9.8 %copy-start.3 = (f32[2,8,128]{2,1,0:T(8,128)S(1)}, f32[2,8,128]{2,1,0:T(8,128)}, u32[]{:S(2)}) copy-start(f32[2,8,128]{2,1,0:T(8,128)} %param.10) | copy-start | bytes 24580
  18.4 18.6 %collective-permute-start = (bf16[128,4,512]{2,0,1:T(8,128)(2,1)S(1)}, bf16[128,4,512]{2,0,1:T(8,128)(2,1)S(1)}, u32[]{:S(2)}, u32[]{:S(2)}) collective-permute-start(bf16[128,4,512]{2,0,1:T(8,128)(2,1)S(1)} %get-tuple-element.30), channel_id=1, source_target_pairs={{16,0},{32,16},{48,32},{64,48},{80,64},{96,80},{112,96},{17,1},{33... | collective-permute-start | bytes 1572872 | tf_op jit(solution)/shard_map/ppermute | solution.py:13
  21.7 22.8 %collective-permute-start.1 = (bf16[128,4,512]{2,0,1:T(8,128)(2,1)S(1)}, bf16[128,4,512]{2,0,1:T(8,128)(2,1)S(1)}, u32[]{:S(2)}, u32[]{:S(2)}) collective-permute-start(bf16[128,4,512]{2,0,1:T(8,128)(2,1)S(1)} %get-tuple-element.29), channel_id=1, source_target_pairs={{0,16},{16,32},{32,48},{48,64},{64,80},{80,96},{96,112},{1,17},{17... | collective-permute-start | bytes 1572872 | tf_op jit(solution)/shard_map/ppermute | solution.py:13
  48.9 10.5 %collective-permute-start.2 = (bf16[128,4,512]{2,0,1:T(8,128)(2,1)S(1)}, bf16[128,4,512]{2,0,1:T(8,128)(2,1)S(1)}, u32[]{:S(2)}, u32[]{:S(2)}) collective-permute-start(bf16[128,4,512]{2,0,1:T(8,128)(2,1)S(1)} %get-tuple-element.28), channel_id=1, source_target_pairs={{16,0},{32,16},{48,32},{64,48},{80,64},{96,80},{112,96},{17,1},{33... | collective-permute-start | bytes 1572872 | tf_op jit(solution)/shard_map/ppermute | solution.py:13
  50.8 9.8 %collective-permute-start.3 = (bf16[128,4,512]{2,0,1:T(8,128)(2,1)S(1)}, bf16[128,4,512]{2,0,1:T(8,128)(2,1)S(1)}, u32[]{:S(2)}, u32[]{:S(2)}) collective-permute-start(bf16[128,4,512]{2,0,1:T(8,128)(2,1)S(1)} %get-tuple-element.27), channel_id=1, source_target_pairs={{0,16},{16,32},{32,48},{48,64},{64,80},{80,96},{96,112},{1,17},{17... | collective-permute-start | bytes 1572872 | tf_op jit(solution)/shard_map/ppermute | solution.py:13
  90.2 91.2 %copy-start.4 = (s32[8]{0:T(128)S(1)}, s32[8]{0:T(128)}, u32[]{:S(2)}) copy-start(s32[8]{0:T(128)} %param.11) | copy-start | bytes 100
  90.2 460.7 %all-gather.3.cloned.1.call-start = ((), (), s32[]{:S(2)}) async-start(), calls=%async_computation.2 | async-start | bytes 71303168 | tf_op jit(solution)/shard_map/all_gather | solution.py:86
  177.5 7.1 copy-start.2
  584.2 1.9 copy-start.1
Sparse Core Ops, SparseCore 0:
  90.3 87.0 reduce-scatter.1
  181.6 369.2 all-gather.2
